TPU v7x, 32 devices: a whole 2x2x4 slice. The times are simulated.
32 devices in a mesh: dp: 4 (over z), ctx: 8 (over y, x, core).
Axes of the slice: x: 2, y: 2, z: 4, core: 2. Of those that a mesh axis runs over, the one named last changes fastest.
Arguments:
- queries: bfloat16 [4, 1024, 1792], P('dp', 'ctx'), may hold values from -40 to 40
- keys: bfloat16 [4, 1024, 256], P('dp', 'ctx'), may hold values from -8 to 8
- values: bfloat16 [4, 1024, 256], P('dp', 'ctx'), may hold values from -6 to 6
- spikes: int32 [4, 1024, 2], P('dp', 'ctx'), may hold values from 0 to 3
- window_lengths: int32 [2], replicated, may hold values from 128 to 256, as said below
- gain: float32 [1792], replicated, may hold values from 0.1 to 1.9
- cotangent: bfloat16 [4, 1024, 1792], P('dp', 'ctx'), may hold values from -6 to 6
Outputs:
- mixed: bfloat16 [4, 1024, 1792], P('dp', 'ctx')
- d_queries: bfloat16 [4, 1024, 1792], P('dp', 'ctx')
- keys_gradient: bfloat16 [4, 1024, 256], P('dp', 'ctx')
- values_gradient: bfloat16 [4, 1024, 256], P('dp', 'ctx')
- d_gain: float32 [1792], replicated
Inputs may be any that keep to these rules, and one draw needn't show every extreme that they name: `window_lengths`: in every draw one key-value head has a look-back of exactly 256.
All inputs are finite; a program needn't handle non-finite values.
Results may differ from a plain program's by a relative error of at most 0.012.
The roundings to bfloat16 on the way count: a program that leaves them out, or rounds other values in their place, can miss the bound.
Values may be sent and summed in bfloat16 or wider, within the bound.
No kernel may reach another device: no remote copies, remote signals or barrier semaphores. Data moves between devices by JAX's collectives and lax.ppermute only.
A program may use at most 64 MiB of HBM per device.

v0:
```python
import math
import jax
import jax.numpy as jnp
from jax import lax
from jax.sharding import PartitionSpec as P

QUERY_HEADS = 14
KEY_VALUE_HEADS = 2
HEAD_SIZE = 128
WINDOW_REACH = 256
epsilon = 1e-05


def carried_in(part, axis, combine, identity, reverse):
    count = lax.axis_size(axis)
    place = lax.axis_index(axis)
    ahead = count - 1 - place if reverse else place
    gathered = lax.all_gather(part, axis)
    state = jnp.zeros_like(part) + jnp.asarray(identity, part.dtype)

    def one(step, state):
        source = count - 1 - step if reverse else step
        return combine(state, lax.dynamic_index_in_dim(gathered, source, 0, False))

    return lax.fori_loop(0, ahead, one, state)


def shifted(block, axis, distance):
    devices = range(lax.axis_size(axis))
    route = [(i - distance, i) for i in devices if i - distance in devices]
    return lax.ppermute(block, axis, route)


def combine_sum(earlier, later):
    return earlier + later


def per_device(queries, keys, values, spikes, window_lengths, gain, cotangent):
    batch_inputs = queries.shape[0]
    token_rows = queries.shape[1]
    group_size = QUERY_HEADS // KEY_VALUE_HEADS
    reach = (WINDOW_REACH + token_rows - 2) // token_rows
    padding_rows = reach * token_rows
    window_rows = (reach + 1) * token_rows
    scale = HEAD_SIZE ** (-0.5)
    key_value_width = KEY_VALUE_HEADS * HEAD_SIZE
    query_heads = queries.reshape(batch_inputs, token_rows, KEY_VALUE_HEADS, group_size, HEAD_SIZE)
    key_heads = keys.reshape(batch_inputs, token_rows, KEY_VALUE_HEADS, HEAD_SIZE)
    value_heads = values.reshape(batch_inputs, token_rows, KEY_VALUE_HEADS, HEAD_SIZE)
    token_counts = spikes.astype(jnp.float32)[..., None]
    spiked = (value_heads.astype(jnp.float32) * token_counts).astype(jnp.bfloat16)
    local_state = jnp.einsum(
        "nrgd,nrge->ngde", key_heads, spiked, preferred_element_type=jnp.float32
    )
    prior = carried_in(local_state, "ctx", combine_sum, jnp.zeros_like(local_state), False)
    prior_half = prior.astype(jnp.bfloat16)
    earlier = []
    for distance in range(reach, 0, -1):
        earlier.append(shifted((keys, values), "ctx", distance))
    key_window = jnp.concatenate([piece[0] for piece in earlier] + [keys], axis=1).reshape(
        batch_inputs, window_rows, KEY_VALUE_HEADS, HEAD_SIZE
    )
    value_window = jnp.concatenate([piece[1] for piece in earlier] + [values], axis=1).reshape(
        batch_inputs, window_rows, KEY_VALUE_HEADS, HEAD_SIZE
    )
    row_idx = jnp.arange(token_rows)
    causal = (row_idx[:, None] >= row_idx[None, :]).astype(jnp.float32)
    key_idx = jnp.arange(window_rows)
    distance_back = row_idx[:, None] + padding_rows - key_idx[None, :]
    key_pos = lax.axis_index("ctx") * token_rows + key_idx - padding_rows
    visible = (
        (distance_back[None] >= 0)
        & (distance_back[None] < window_lengths[:, None, None])
        & (key_pos >= 0)[None, None, :]
    )
    lin_half = (
        jnp.einsum("nrghd,nsgd->nghrs", query_heads, key_heads, preferred_element_type=jnp.float32)
        * causal
    ).astype(jnp.bfloat16)
    linear = jnp.einsum("nghrs,nsge->nrghe", lin_half, spiked, preferred_element_type=jnp.float32)
    linear = linear + jnp.einsum(
        "nrghd,ngde->nrghe", query_heads, prior_half, preferred_element_type=jnp.float32
    )
    root = jnp.sqrt(jnp.mean(linear * linear, axis=-1, keepdims=True) + epsilon)
    normed = linear / root
    head_gains = gain.reshape(KEY_VALUE_HEADS, group_size, HEAD_SIZE)
    scores = (
        jnp.einsum("nrghd,nmgd->nghrm", query_heads, key_window, preferred_element_type=jnp.float32)
        * scale
    )
    scores = jnp.where(visible[None, :, None], scores, -1e30)
    top = jnp.max(scores, axis=-1, keepdims=True)
    expo = jnp.exp(scores - top)
    probs = expo / jnp.sum(expo, axis=-1, keepdims=True)
    probs_half = probs.astype(jnp.bfloat16)
    window_out = jnp.einsum(
        "nghrm,nmgd->nrghd", probs_half, value_window, preferred_element_type=jnp.float32
    )
    mixed = (
        (head_gains * normed + window_out)
        .astype(jnp.bfloat16)
        .reshape(batch_inputs, token_rows, QUERY_HEADS * HEAD_SIZE)
    )
    head_gradients = cotangent.reshape(
        batch_inputs, token_rows, KEY_VALUE_HEADS, group_size, HEAD_SIZE
    )
    grad_wide = head_gradients.astype(jnp.float32)
    total_tokens = batch_inputs * lax.axis_size("dp") * token_rows * lax.axis_size("ctx")
    gain_local = jnp.sum(grad_wide * normed, axis=(0, 1)).reshape(
        QUERY_HEADS * HEAD_SIZE
    ) / math.sqrt(total_tokens)
    d_gain = lax.psum(gain_local, ("dp", "ctx"))
    scaled = grad_wide * head_gains
    d_linear = (
        (scaled - normed * jnp.mean(scaled * normed, axis=-1, keepdims=True)) / root
    ).astype(jnp.bfloat16)
    suffix_local = jnp.einsum(
        "nrghd,nrghe->ngde", query_heads, d_linear, preferred_element_type=jnp.float32
    )
    later = carried_in(suffix_local, "ctx", combine_sum, jnp.zeros_like(suffix_local), True)
    later_half = later.astype(jnp.bfloat16)
    back_half = (
        jnp.einsum("nrghe,nsge->nghrs", d_linear, spiked, preferred_element_type=jnp.float32)
        * causal
    ).astype(jnp.bfloat16)
    lin_dq = jnp.einsum(
        "nrghe,ngde->nrghd", d_linear, prior_half, preferred_element_type=jnp.float32
    )
    lin_dq = lin_dq + jnp.einsum(
        "nghrs,nsgd->nrghd", back_half, key_heads, preferred_element_type=jnp.float32
    )
    linear_key_gradient = jnp.einsum(
        "nghrs,nrghd->nsgd", back_half, query_heads, preferred_element_type=jnp.float32
    )
    linear_key_gradient = linear_key_gradient + jnp.einsum(
        "nsge,ngde->nsgd", spiked, later_half, preferred_element_type=jnp.float32
    )
    d_spiked = jnp.einsum(
        "nghrs,nrghe->nsge", lin_half, d_linear, preferred_element_type=jnp.float32
    )
    d_spiked = d_spiked + jnp.einsum(
        "nsgd,ngde->nsge", key_heads, later_half, preferred_element_type=jnp.float32
    )
    linear_value_gradient = d_spiked * token_counts
    grad_probs = jnp.einsum(
        "nrghd,nmgd->nghrm", head_gradients, value_window, preferred_element_type=jnp.float32
    )
    delta = jnp.transpose(jnp.sum(grad_wide * window_out, axis=-1), (0, 2, 3, 1))
    grad_scores = (probs * (grad_probs - delta[..., None]) * scale).astype(jnp.bfloat16)
    window_dq = jnp.einsum(
        "nghrm,nmgd->nrghd", grad_scores, key_window, preferred_element_type=jnp.float32
    )
    key_grad_window = jnp.einsum(
        "nghrm,nrghd->nmgd", grad_scores, query_heads, preferred_element_type=jnp.float32
    ).reshape(batch_inputs, window_rows, key_value_width)
    value_grad_window = jnp.einsum(
        "nghrm,nrghd->nmgd", probs_half, head_gradients, preferred_element_type=jnp.float32
    ).reshape(batch_inputs, window_rows, key_value_width)
    received_k = jnp.zeros((batch_inputs, token_rows, key_value_width), jnp.float32)
    received_v = jnp.zeros((batch_inputs, token_rows, key_value_width), jnp.float32)
    for distance in range(1, reach + 1):
        start_row = (reach - distance) * token_rows
        sent_k = key_grad_window[:, start_row : start_row + token_rows]
        sent_v = value_grad_window[:, start_row : start_row + token_rows]
        got_k, got_v = shifted((sent_k, sent_v), "ctx", -distance)
        received_k = received_k + got_k
        received_v = received_v + got_v
    own_k = key_grad_window[:, padding_rows:]
    own_v = value_grad_window[:, padding_rows:]
    d_queries = (
        (lin_dq + window_dq)
        .astype(jnp.bfloat16)
        .reshape(batch_inputs, token_rows, QUERY_HEADS * HEAD_SIZE)
    )
    keys_gradient = (
        linear_key_gradient.reshape(batch_inputs, token_rows, key_value_width) + own_k + received_k
    ).astype(jnp.bfloat16)
    values_gradient = (
        linear_value_gradient.reshape(batch_inputs, token_rows, key_value_width)
        + own_v
        + received_v
    ).astype(jnp.bfloat16)
    return (mixed, d_queries, keys_gradient, values_gradient, d_gain)


def solution(mesh):
    placed = (
        P("dp", "ctx", None),
        P("dp", "ctx", None),
        P("dp", "ctx", None),
        P("dp", "ctx", None),
        P(),
        P(),
        P("dp", "ctx", None),
    )
    return jax.shard_map(
        per_device,
        mesh=mesh,
        in_specs=placed,
        out_specs=(
            P("dp", "ctx", None),
            P("dp", "ctx", None),
            P("dp", "ctx", None),
            P("dp", "ctx", None),
            P(),
        ),
        check_vma=False,
    )
```

profile of v0, /device:TPU:0, one launch (start us, length us, event | category | flops | bytes accessed | tf_op | source)
XLA Modules:
  0.0 137.0 jit_solution(10712127279275393058)
XLA Ops:
  7.2 1.0 copy.113
  8.2 4.8 %collective-permute-start.2 = (bf16[1,128,256]{1,2,0:T(8,128)(2,1)S(1)}, bf16[1,128,256]{1,2,0:T(8,128)(2,1)S(1)}, u32[]{:S(2)}, u32[]{:S(2)}) collective-permute-start(bf16[1,128,256]{1,2,0:T(8,128)(2,1)S(1)} %copy.113), channel_id=1, source_target_pairs={{0,2},{1,3},{2,4},{3,5},{4,6},{5,7},{8,10},{9,11},{10,12},{11,13},... | collective-permute-start | bytes 196616 | tf_op jit(solution)/shard_map/ppermute | solution.py:31
  13.1 1.5 %collective-permute-start.3 = (bf16[1,128,256]{1,2,0:T(8,128)(2,1)S(1)}, bf16[1,128,256]{1,2,0:T(8,128)(2,1)S(1)}, u32[]{:S(2)}, u32[]{:S(2)}) collective-permute-start(bf16[1,128,256]{1,2,0:T(8,128)(2,1)S(1)} %copy.113), channel_id=1, source_target_pairs={{0,1},{1,2},{2,3},{3,4},{4,5},{5,6},{6,7},{8,9},{9,10},{10,11},{11... | collective-permute-start | bytes 196616 | tf_op jit(solution)/shard_map/ppermute | solution.py:31
  14.5 3.9 %collective-permute-start = (bf16[1,128,256]{2,1,0:T(8,128)(2,1)}, bf16[1,128,256]{2,1,0:T(8,128)(2,1)S(1)}, u32[]{:S(2)}, u32[]{:S(2)}) collective-permute-start(bf16[1,128,256]{2,1,0:T(8,128)(2,1)} %param.13), channel_id=1, source_target_pairs={{0,2},{1,3},{2,4},{3,5},{4,6},{5,7},{8,10},{9,11},{10,12},{11,13},... | collective-permute-start | bytes 196616 | tf_op jit(solution)/shard_map/ppermute | solution.py:31
  18.4 3.2 %collective-permute-start.1 = (bf16[1,128,256]{2,1,0:T(8,128)(2,1)}, bf16[1,128,256]{2,1,0:T(8,128)(2,1)S(1)}, u32[]{:S(2)}, u32[]{:S(2)}) collective-permute-start(bf16[1,128,256]{2,1,0:T(8,128)(2,1)} %param.13), channel_id=1, source_target_pairs={{0,1},{1,2},{2,3},{3,4},{4,5},{5,6},{6,7},{8,9},{9,10},{10,11},{11... | collective-permute-start | bytes 196616 | tf_op jit(solution)/shard_map/ppermute | solution.py:31
  21.6 0.9 reshape.302
  22.6 0.9 reshape.284
  23.4 0.7 convert_bitcast_fusion
  24.5 0.8 copy.108
  25.4 1.3 copy.101
  26.9 1.5 %and_and_fusion = pred[2,128,384]{1,2,0:T(8,128)(4,1)} fusion(s32[128,384]{0,1:T(8,128)S(1)} %iota_subtract_fusion, s32[2]{0:T(128)} %param.15, pred[384]{0:T(512)(128)(4,1)S(1)} %add_compare_fusion, pred[128,384]{0,1:T(8,128)(4,1)S(1)} %broadcast_compare_fusion), kind=kLoop, calls=%fused_computation.54 | loop fusion | flops 294912 | bytes 344456 | tf_op jit(solution)/shard_map/and | solution.py:72
  28.3 1.1 fusion.23
  29.5 1.1 copy.119
  30.6 1.0 copy.124
  31.6 0.8 copy.112
  32.5 1.6 %fusion.5 = (f32[2,7,128]{2,1,0:T(8,128)S(1)}, f32[2,384,128,7]{2,1,3,0:T(8,128)S(1)}) fusion(pred[2,128,384]{1,2,0:T(8,128)(4,1)} %and_and_fusion, bf16[384,2,128,1]{0,2,3,1:T(8,128)(2,1)S(1)} %bitcast.263, bf16[128,2,7,128]{0,3,2,1:T(8,128)(2,1)S(1)} %bitcast.255), kind=kOutput, calls=%fused_computation.10 | convolution fusion | flops 178223360 | bytes 3513344 | tf_op jit(solution)/shard_map/nrghd,nmgd->nghrm/dot_general | solution.py:88
  34.7 0.9 fusion.7
  35.6 0.7 fusion.47
  36.4 1.7 %copy.195 = f32[1,128,256]{2,1,0:T(8,128)} copy(f32[1,128,256]{1,2,0:T(8,128)} %get-tuple-element.146) | data formatting | bytes 262144
  38.0 1.3 collective-permute-start.6
  39.3 1.7 %copy.196 = f32[1,128,256]{2,1,0:T(8,128)} copy(f32[1,128,256]{1,2,0:T(8,128)} %get-tuple-element.147) | data formatting | bytes 262144
  41.0 1.3 collective-permute-start.7
  42.3 0.8 copy.194
  43.0 7.1 %all-gather.5.cloned.1.call-done = f32[16,128,128]{2,1,0:T(8,128)} async-done(((f32[2,128,128]{2,1,0:T(8,128)}), f32[16,128,128]{2,1,0:T(8,128)}) %all-gather.5.cloned.1.call-update) | async-done | bytes 1048592 | tf_op jit(solution)/shard_map/all_gather | solution.py:18
  50.5 1.4 %multiply_reduce_fusion.3 = (f32[128,2,7]{0,2,1:T(8,128)S(1)}, f32[1,128,2,7,128]{1,4,3,2,0:T(8,128)S(1)}) fusion(f32[1,128,2,7,128]{1,4,3,2,0:T(8,128)S(1)} %convolution_bitcast_fusion.3, bf16[2,7,128,128]{2,3,1,0:T(8,128)(2,1)} %fusion.23, bf16[128,2,128]{2,0,1:T(8,128)(2,1)} %copy-done.4), kind=kOutput, calls=%fused_computation.48 | convolution fusion | flops 59406592 | bytes 2366464 | tf_op jit(solution)/shard_map/nghrs,nsge->nrghe/dot_general | solution.py:80
  52.0 2.7 %multiply_reduce_fusion = (f32[2,7,128]{2,1,0:T(8,128)}, f32[128,2,7]{0,2,1:T(8,128)S(1)}, f32[128,2,7]{0,2,1:T(8,128)}, bf16[1,128,2,7,128]{1,4,3,2,0:T(8,128)(2,1)}) fusion(f32[1,128,2,7,128]{1,4,3,2,0:T(8,128)S(1)} %bitcast.260, f32[1,128,2,7,128]{1,4,3,2,0:T(8,128)S(1)} %get-tuple-element.152, f32[128,2,7]{0,2,1:T(8,128)S(1)} %add_sqrt_fusion, ...), kind=kOutput, calls=%fused_computation.43 | convolution fusion | flops 182119168 | bytes 5391360 | tf_op jit(solution)/shard_map/nghrm,nmgd->nrghd/dot_general | solution.py:96
  55.3 0.8 copy.130
  56.2 2.9 %fusion.6 = bf16[2,7,128,384]{2,3,1,0:T(8,128)(2,1)S(1)} fusion(bf16[384,2,128,1]{0,2,3,1:T(8,128)(2,1)S(1)} %bitcast.276, bf16[128,2,7,128]{0,3,2,1:T(8,128)(2,1)S(1)} %bitcast.270, f32[2,7,128]{2,1,0:T(8,128)S(1)} %bitcast.277, f32[2,7,128]{2,1,0:T(8,128)S(1)} %copy-done.27, f32[2,7,128]{2,1,0:T(8,128)S(1)} %get-tuple-element.153, ...), kind=kOutput, calls=%fused_computation.11 | convolution fusion | flops 181665792 | bytes 4903936 | tf_op jit(solution)/shard_map/nrghd,nmgd->nghrm/dot_general | solution.py:145
  59.7 0.7 fusion.48
  60.3 1.7 %copy.192 = f32[1,128,256]{2,1,0:T(8,128)} copy(f32[1,128,256]{1,2,0:T(8,128)} %get-tuple-element.149) | data formatting | bytes 262144
  62.0 1.3 collective-permute-start.4
  63.3 0.8 copy.193
  64.0 1.3 collective-permute-start.5
  65.3 0.7 copy.191
  66.9 1.2 fusion.20
  68.1 2.0 %copy.146 = bf16[1,128,1792]{2,1,0:T(8,128)(2,1)} copy(bf16[1,128,1792]{1,2,0:T(8,128)(2,1)} %bitcast.262) | data formatting | bytes 917504
  70.1 2.0 %copy.145 = bf16[1,128,1792]{2,1,0:T(8,128)(2,1)} copy(bf16[1,128,1792]{1,2,0:T(8,128)(2,1)} %bitcast.271) | data formatting | bytes 917504
  72.2 46.7 %psum.7 = f32[1792]{0:T(1024)} all-reduce(f32[1792]{0:T(1024)S(1)} %div.45), channel_id=1, replica_groups=mesh['dp'=4,'ctx'=8] {'dp','ctx'}, use_global_device_ids=true, to_apply=%region_10.11 | all-reduce | flops 1792 | bytes 14336 | tf_op jit(solution)/shard_map/psum | solution.py:112
  119.5 6.8 %while.23 = (s32[]{:T(128)}, f32[1,2,128,128]{3,2,1,0:T(8,128)S(1)}, s32[]{:T(128)}, f32[8,1,2,128,128]{4,3,2,1,0:T(8,128)}, s32[]{:T(128)}, /*index=5*/s32[]{:T(128)}, s32[]{:T(128)}, s32[]{:T(128)}) while((s32[]{:T(128)}, f32[1,2,128,128]{3,2,1,0:T(8,128)S(1)}, s32[]{:T(128)}, f32[8,1,2,128,128]{4,3,2,1,0:T(8,128)}, s32[]{:T(128)}, ...), condition=%wide.region_8.9_spmd, body=%wide.region_7.8_spmd.sunk | while | flops 32774 | bytes 393351 | solution.py:25
  119.5 0.9 bitcast_add_fusion.5
  120.5 0.9 bitcast_add_fusion.5
  121.5 0.9 bitcast_add_fusion.5
  122.4 0.9 bitcast_add_fusion.5
  123.4 0.9 bitcast_add_fusion.5
  124.3 0.9 bitcast_add_fusion.5
  125.3 0.9 bitcast_add_fusion.5
  126.9 1.6 %add_convert_fusion.1 = bf16[1,128,256]{2,1,0:T(8,128)(2,1)} fusion(f32[1,128,256]{2,1,0:T(8,128)} %collective-permute-done.6, f32[1,128,256]{2,1,0:T(8,128)} %collective-permute-done.7, f32[1,128,256]{2,1,0:T(8,128)S(1)} %copy.142, f32[1,128,256]{2,1,0:T(8,128)S(1)} %copy-done.16), kind=kLoop, calls=%fused_computation.60 | loop fusion | flops 131072 | bytes 589824 | tf_op jit(solution)/shard_map/convert_element_type | solution.py:182
  128.6 1.6 %add_convert_fusion.2 = bf16[1,128,256]{2,1,0:T(8,128)(2,1)} fusion(f32[1,128,256]{2,1,0:T(8,128)} %collective-permute-done.4, f32[1,128,256]{2,1,0:T(8,128)} %collective-permute-done.5, f32[1,128,256]{2,1,0:T(8,128)S(1)} %copy.134, f32[1,128,256]{2,1,0:T(8,128)S(1)} %copy-done.17), kind=kLoop, calls=%fused_computation.61 | loop fusion | flops 131072 | bytes 589824 | tf_op jit(solution)/shard_map/convert_element_type | solution.py:177
  (107 shorter events, 5.0 us)
Async XLA Ops:
  7.2 22.3 %copy-start.3 = (bf16[1,128,1792]{2,1,0:T(8,128)(2,1)S(1)}, bf16[1,128,1792]{2,1,0:T(8,128)(2,1)}, u32[]{:S(2)}) copy-start(bf16[1,128,1792]{2,1,0:T(8,128)(2,1)} %param.17) | copy-start | bytes 1376260
  7.2 43.0 %all-gather.5.cloned.1.call-start = ((), (), s32[]{:S(2)}) async-start(), calls=%async_computation | async-start | bytes 1179648 | tf_op jit(solution)/shard_map/all_gather | solution.py:18
  8.2 24.2 %collective-permute-start.2 = (bf16[1,128,256]{1,2,0:T(8,128)(2,1)S(1)}, bf16[1,128,256]{1,2,0:T(8,128)(2,1)S(1)}, u32[]{:S(2)}, u32[]{:S(2)}) collective-permute-start(bf16[1,128,256]{1,2,0:T(8,128)(2,1)S(1)} %copy.113), channel_id=1, source_target_pairs={{0,2},{1,3},{2,4},{3,5},{4,6},{5,7},{8,10},{9,11},{10,12},{11,13},... | collective-permute-start | bytes 196616 | tf_op jit(solution)/shard_map/ppermute | solution.py:31
  13.1 19.4 %collective-permute-start.3 = (bf16[1,128,256]{1,2,0:T(8,128)(2,1)S(1)}, bf16[1,128,256]{1,2,0:T(8,128)(2,1)S(1)}, u32[]{:S(2)}, u32[]{:S(2)}) collective-permute-start(bf16[1,128,256]{1,2,0:T(8,128)(2,1)S(1)} %copy.113), channel_id=1, source_target_pairs={{0,1},{1,2},{2,3},{3,4},{4,5},{5,6},{6,7},{8,9},{9,10},{10,11},{11... | collective-permute-start | bytes 196616 | tf_op jit(solution)/shard_map/ppermute | solution.py:31
  14.5 17.0 %collective-permute-start = (bf16[1,128,256]{2,1,0:T(8,128)(2,1)}, bf16[1,128,256]{2,1,0:T(8,128)(2,1)S(1)}, u32[]{:S(2)}, u32[]{:S(2)}) collective-permute-start(bf16[1,128,256]{2,1,0:T(8,128)(2,1)} %param.13), channel_id=1, source_target_pairs={{0,2},{1,3},{2,4},{3,5},{4,6},{5,7},{8,10},{9,11},{10,12},{11,13},... | collective-permute-start | bytes 196616 | tf_op jit(solution)/shard_map/ppermute | solution.py:31
  18.4 13.2 %collective-permute-start.1 = (bf16[1,128,256]{2,1,0:T(8,128)(2,1)}, bf16[1,128,256]{2,1,0:T(8,128)(2,1)S(1)}, u32[]{:S(2)}, u32[]{:S(2)}) collective-permute-start(bf16[1,128,256]{2,1,0:T(8,128)(2,1)} %param.13), channel_id=1, source_target_pairs={{0,1},{1,2},{2,3},{3,4},{4,5},{5,6},{6,7},{8,9},{9,10},{10,11},{11... | collective-permute-start | bytes 196616 | tf_op jit(solution)/shard_map/ppermute | solution.py:31
  23.4 8.1 %copy-start.7 = (bf16[128,2,128]{2,1,0:T(2,128)(2,1)}, bf16[128,2,128]{2,1,0:T(2,128)(2,1)S(1)}, u32[]{:S(2)}) copy-start(bf16[128,2,128]{2,1,0:T(2,128)(2,1)S(1)} %reshape.284) | copy-start | bytes 196612
  24.1 1.2 copy-start.23
  24.2 1.2 copy-start.4
  24.5 7.1 %copy-start.28 = (f32[1792]{0:T(1024)S(1)}, f32[1792]{0:T(1024)}, u32[]{:S(2)}) copy-start(f32[1792]{0:T(1024)} %param.16) | copy-start | bytes 21508
  24.5 7.1 %copy-start.20 = (bf16[1,128,256]{2,1,0:T(8,128)(2,1)S(1)}, bf16[1,128,256]{2,1,0:T(8,128)(2,1)}, u32[]{:S(2)}) copy-start(bf16[1,128,256]{2,1,0:T(8,128)(2,1)} %param.13) | copy-start | bytes 196612
  25.3 94.2 %all-gather.7.cloned.1.call-start = ((), (), s32[]{:S(2)}) async-start(), calls=%async_computation.1 | async-start | bytes 1179648 | tf_op jit(solution)/shard_map/all_gather | solution.py:18
  26.9 5.6 %copy-start.12 = (bf16[128,2,128,1]{0,2,3,1:T(8,128)(2,1)}, bf16[128,2,128,1]{0,2,3,1:T(8,128)(2,1)S(1)}, u32[]{:S(2)}) copy-start(bf16[128,2,128,1]{0,2,3,1:T(8,128)(2,1)S(1)} %copy.163) | copy-start | bytes 196612
  28.3 4.2 %copy-start.14 = (f32[128,128]{0,1:T(8,128)}, f32[128,128]{0,1:T(8,128)S(1)}, u32[]{:S(2)}) copy-start(f32[128,128]{0,1:T(8,128)S(1)} %fusion.38) | copy-start | bytes 196612
  31.6 2.5 %copy-start.9 = (pred[2,128,384]{1,2,0:T(8,128)(4,1)S(1)}, pred[2,128,384]{1,2,0:T(8,128)(4,1)}, u32[]{:S(2)}) copy-start(pred[2,128,384]{1,2,0:T(8,128)(4,1)} %and_and_fusion) | copy-start | bytes 294916
  32.5 2.2 %copy-start.18 = (bf16[1,128,1792]{1,2,0:T(8,128)(2,1)S(1)}, bf16[1,128,1792]{1,2,0:T(8,128)(2,1)}, u32[]{:S(2)}) copy-start(bf16[1,128,1792]{1,2,0:T(8,128)(2,1)} %copy.124) | copy-start | bytes 1376260
  34.1 17.9 %copy-start = (f32[2,384,128,7]{2,1,3,0:T(8,128)}, f32[2,384,128,7]{2,1,3,0:T(8,128)S(1)}, u32[]{:S(2)}) copy-start(f32[2,384,128,7]{2,1,3,0:T(8,128)S(1)} %get-tuple-element.154) | copy-start | bytes 8257540
  34.7 0.9 copy-start.25
  38.0 88.9 %collective-permute-start.6 = (f32[1,128,256]{2,1,0:T(8,128)}, f32[1,128,256]{2,1,0:T(8,128)}, u32[]{:S(2)}, u32[]{:S(2)}) collective-permute-start(f32[1,128,256]{2,1,0:T(8,128)} %copy.195), channel_id=1, source_target_pairs={{1,0},{2,1},{3,2},{4,3},{5,4},{6,5},{7,6},{9,8},{10,9},{11,10},{12... | collective-permute-start | bytes 393224 | tf_op jit(solution)/shard_map/ppermute | solution.py:31
  41.0 85.9 %collective-permute-start.7 = (f32[1,128,256]{2,1,0:T(8,128)}, f32[1,128,256]{2,1,0:T(8,128)}, u32[]{:S(2)}, u32[]{:S(2)}) collective-permute-start(f32[1,128,256]{2,1,0:T(8,128)} %copy.196), channel_id=1, source_target_pairs={{2,0},{3,1},{4,2},{5,3},{6,4},{7,5},{10,8},{11,9},{12,10},{13,11},... | collective-permute-start | bytes 393224 | tf_op jit(solution)/shard_map/ppermute | solution.py:31
  50.2 1.8 %copy-start.2 = (f32[1,128,1792]{1,2,0:T(8,128)S(1)}, f32[1,128,1792]{1,2,0:T(8,128)}, u32[]{:S(2)}) copy-start(f32[1,128,1792]{1,2,0:T(8,128)} %copy.119) | copy-start | bytes 2752516
  50.2 1.8 %copy-start.10 = (pred[2,128,384]{1,2,0:T(8,128)(4,1)S(1)}, pred[2,128,384]{1,2,0:T(8,128)(4,1)}, u32[]{:S(2)}) copy-start(pred[2,128,384]{1,2,0:T(8,128)(4,1)} %and_and_fusion) | copy-start | bytes 294916
  50.2 1.8 %copy-start.21 = (bf16[1,384,256]{1,2,0:T(8,128)(2,1)S(1)}, bf16[1,384,256]{1,2,0:T(8,128)(2,1)}, u32[]{:S(2)}) copy-start(bf16[1,384,256]{1,2,0:T(8,128)(2,1)} %copy.112) | copy-start | bytes 589828
  50.2 1.8 %copy-start.26 = (f32[2,7,128]{2,1,0:T(8,128)S(1)}, f32[2,7,128]{2,1,0:T(8,128)}, u32[]{:S(2)}) copy-start(f32[2,7,128]{2,1,0:T(8,128)} %copy-done.25) | copy-start | bytes 21508
  54.7 1.4 %copy-start.11 = (pred[2,128,384]{1,2,0:T(8,128)(4,1)S(1)}, pred[2,128,384]{1,2,0:T(8,128)(4,1)}, u32[]{:S(2)}) copy-start(pred[2,128,384]{1,2,0:T(8,128)(4,1)} %and_and_fusion) | copy-start | bytes 294916
  54.7 1.4 %copy-start.19 = (bf16[1,128,1792]{1,2,0:T(8,128)(2,1)S(1)}, bf16[1,128,1792]{1,2,0:T(8,128)(2,1)}, u32[]{:S(2)}) copy-start(bf16[1,128,1792]{1,2,0:T(8,128)(2,1)} %copy.124) | copy-start | bytes 1376260
  54.7 1.4 %copy-start.22 = (bf16[1,384,256]{1,2,0:T(8,128)(2,1)S(1)}, bf16[1,384,256]{1,2,0:T(8,128)(2,1)}, u32[]{:S(2)}) copy-start(bf16[1,384,256]{1,2,0:T(8,128)(2,1)} %copy.112) | copy-start | bytes 589828
  54.7 1.4 %copy-start.27 = (f32[2,7,128]{2,1,0:T(8,128)S(1)}, f32[2,7,128]{2,1,0:T(8,128)}, u32[]{:S(2)}) copy-start(f32[2,7,128]{2,1,0:T(8,128)} %copy-done.25) | copy-start | bytes 21508
  54.7 1.5 %copy-start.30 = (f32[128,2,7]{0,2,1:T(8,128)S(1)}, f32[128,2,7]{0,2,1:T(8,128)}, u32[]{:S(2)}) copy-start(f32[128,2,7]{0,2,1:T(8,128)} %get-tuple-element.127) | copy-start | bytes 21508
  59.1 7.0 %copy-start.5 = (bf16[128,2,128]{2,0,1:T(8,128)(2,1)S(1)}, bf16[128,2,128]{2,0,1:T(8,128)(2,1)}, u32[]{:S(2)}) copy-start(bf16[128,2,128]{2,0,1:T(8,128)(2,1)} %copy-done.4) | copy-start | bytes 196612
  59.1 7.0 %copy-start.15 = (f32[128,128]{0,1:T(8,128)S(1)}, f32[128,128]{0,1:T(8,128)}, u32[]{:S(2)}) copy-start(f32[128,128]{0,1:T(8,128)} %copy-done.14) | copy-start | bytes 196612
  59.1 7.3 %copy-start.13 = (bf16[128,2,128,1]{0,2,3,1:T(8,128)(2,1)S(1)}, bf16[128,2,128,1]{0,2,3,1:T(8,128)(2,1)}, u32[]{:S(2)}) copy-start(bf16[128,2,128,1]{0,2,3,1:T(8,128)(2,1)} %copy-done.12) | copy-start | bytes 196612
  62.0 66.6 %collective-permute-start.4 = (f32[1,128,256]{2,1,0:T(8,128)}, f32[1,128,256]{2,1,0:T(8,128)}, u32[]{:S(2)}, u32[]{:S(2)}) collective-permute-start(f32[1,128,256]{2,1,0:T(8,128)} %copy.192), channel_id=1, source_target_pairs={{1,0},{2,1},{3,2},{4,3},{5,4},{6,5},{7,6},{9,8},{10,9},{11,10},{12... | collective-permute-start | bytes 393224 | tf_op jit(solution)/shard_map/ppermute | solution.py:31
  64.0 64.5 %collective-permute-start.5 = (f32[1,128,256]{2,1,0:T(8,128)}, f32[1,128,256]{2,1,0:T(8,128)}, u32[]{:S(2)}, u32[]{:S(2)}) collective-permute-start(f32[1,128,256]{2,1,0:T(8,128)} %copy.193), channel_id=1, source_target_pairs={{2,0},{3,1},{4,2},{5,3},{6,4},{7,5},{10,8},{11,9},{12,10},{13,11},... | collective-permute-start | bytes 393224 | tf_op jit(solution)/shard_map/ppermute | solution.py:31
  66.9 5.3 %copy-start.29 = (f32[2,7,128]{2,1,0:T(8,128)S(1)}, f32[2,7,128]{2,1,0:T(8,128)}, u32[]{:S(2)}) copy-start(f32[2,7,128]{2,1,0:T(8,128)} %get-tuple-element.125) | copy-start | bytes 21508
  66.9 51.9 %copy-start.1 = (bf16[2,7,128,128]{2,3,1,0:T(8,128)(2,1)S(1)}, bf16[2,7,128,128]{2,3,1,0:T(8,128)(2,1)}, u32[]{:S(2)}) copy-start(bf16[2,7,128,128]{2,3,1,0:T(8,128)(2,1)} %fusion.23) | copy-start | bytes 1376260
  70.1 56.1 %copy-start.8 = (bf16[128,2,128]{2,1,0:T(2,128)(2,1)S(1)}, bf16[128,2,128]{2,1,0:T(2,128)(2,1)}, u32[]{:S(2)}) copy-start(bf16[128,2,128]{2,1,0:T(2,128)(2,1)} %copy-done.7) | copy-start | bytes 196612
  70.1 56.1 %copy-start.24 = (f32[128,2]{0,1:T(2,128)S(1)}, f32[128,2]{0,1:T(2,128)}, u32[]{:S(2)}) copy-start(f32[128,2]{0,1:T(2,128)} %copy-done.23) | copy-start | bytes 3076
  72.2 54.4 %copy-start.6 = (bf16[128,2,128]{2,0,1:T(8,128)(2,1)S(1)}, bf16[128,2,128]{2,0,1:T(8,128)(2,1)}, u32[]{:S(2)}) copy-start(bf16[128,2,128]{2,0,1:T(8,128)(2,1)} %copy-done.4) | copy-start | bytes 196612
  118.8 8.1 %copy-start.16 = (f32[1,128,256]{2,1,0:T(8,128)S(1)}, f32[1,128,256]{2,1,0:T(8,128)}, u32[]{:S(2)}) copy-start(f32[1,128,256]{2,1,0:T(8,128)} %copy.194) | copy-start | bytes 393220
  119.1 9.4 %copy-start.17 = (f32[1,128,256]{2,1,0:T(8,128)S(1)}, f32[1,128,256]{2,1,0:T(8,128)}, u32[]{:S(2)}) copy-start(f32[1,128,256]{2,1,0:T(8,128)} %copy.191) | copy-start | bytes 393220
Sparse Core Ops, SparseCore 0:
  25.4 24.7 all-gather.4
  56.2 32.5 all-gather.6
where the time goes:
time: 138 us; the launch traced here: 137 us
  blocking collectives  46.7 us (34%)
  local copies, waits for them, and re-layouts  21.6 us (16%)
  starting transfers between devices  18.6 us (13%)
  matrix products  14.9 us (11%)
  between operations  14.7 us (11%)
  other arithmetic  13.1 us (9%)
  waiting for transfers between devices  7.19 us (5%)
    psum x1, blocking collectives, per_device(): d_gain = lax.psum(gain_local, ('dp', 'ctx'))  46.7 us
    ppermute x8, starting transfers between devices, shifted(): return lax.ppermute(block, axis, route)  18.5 us
    unnamed x73, local copies, waits for them, and re-layouts  14.6 us
    all_gather x2, waiting for transfers between devices, carried_in(): gathered = lax.all_gather(part, axis)  7.14 us
    add x7, other arithmetic, combine_sum(): return earlier + later  6.56 us
    dot_general x1, matrix products, per_device(): jnp.einsum('nrghd,nmgd->nghrm', head_gradients, value_window, preferred_e...  2.9 us
  transfers between devices with their start and end apart: 10, of which 1 were waited for; matrix products, arithmetic and copies ran while one was open for 34% of the time, Pallas kernels for 0%

commit v1 on v0

--- a/solution.py
+++ b/solution.py
@@ -1,3 +1,4 @@
+import functools
 import math
 import jax
 import jax.numpy as jnp
@@ -9,6 +10,13 @@
 HEAD_SIZE = 128
 WINDOW_REACH = 256
 epsilon = 1e-05
+
+
+def files_choose(t0, mesh_name, a_name):
+    return lax.psum(lax.psum(t0, mesh_name), axis_name=a_name)
+
+
+_wait_strips_all = functools.partial(files_choose, mesh_name="ctx", a_name="dp")
 
 
 def carried_in(part, axis, combine, identity, reverse):
@@ -109,7 +117,7 @@
     gain_local = jnp.sum(grad_wide * normed, axis=(0, 1)).reshape(
         QUERY_HEADS * HEAD_SIZE
     ) / math.sqrt(total_tokens)
-    d_gain = lax.psum(gain_local, ("dp", "ctx"))
+    d_gain = _wait_strips_all(gain_local)
     scaled = grad_wide * head_gains
     d_linear = (
         (scaled - normed * jnp.mean(scaled * normed, axis=-1, keepdims=True)) / root

time: 138 us -> 126 us (0.913)
  blocking collectives: 46.7 us -> 33.7 us
    psum x1 -> x2, blocking collectives: 46.7 us -> 33.7 us  [files_choose(): return lax.psum(lax.psum(t0, mesh_name), axis_name=a_name)]
  transfers between devices with their start and end apart: 10 -> 10, of which waited for: 1 -> 1; matrix products, arithmetic and copies ran while one was open for 34% -> 38% of each run, Pallas kernels for 0% -> 0%
where the time goes in v1:
time: 126 us; the launch traced here: 125 us
  blocking collectives  33.7 us (27%)
  local copies, waits for them, and re-layouts  22.3 us (18%)
  starting transfers between devices  18.6 us (15%)
  matrix products  15 us (12%)
  between operations  14.7 us (12%)
  other arithmetic  13.1 us (10%)
  waiting for transfers between devices  7.17 us (6%)
    psum x2, blocking collectives, files_choose(): return lax.psum(lax.psum(t0, mesh_name), axis_name=a_name)  33.7 us
    ppermute x8, starting transfers between devices, shifted(): return lax.ppermute(block, axis, route)  18.5 us
    unnamed x73, local copies, waits for them, and re-layouts  15.3 us
    all_gather x2, waiting for transfers between devices, carried_in(): gathered = lax.all_gather(part, axis)  7.12 us
    add x7, other arithmetic, combine_sum(): return earlier + later  6.56 us
    dot_general x1, matrix products, per_device(): jnp.einsum('nrghd,nmgd->nghrm', head_gradients, value_window, preferred_e...  2.9 us
    dot_general x1, matrix products, per_device(): jnp.einsum('nghrm,nmgd->nrghd', probs_half, value_window, preferred_eleme...  2.67 us
  transfers between devices with their start and end apart: 10, of which 1 were waited for; matrix products, arithmetic and copies ran while one was open for 38% of the time, Pallas kernels for 0%

profile of v1, /device:TPU:0, one launch (start us, length us, event | category | flops | bytes accessed | tf_op | source)
XLA Modules:
  0.0 124.7 jit_solution(10265544468419787564)
XLA Ops:
  7.2 1.0 copy.113
  8.2 4.8 %collective-permute-start.2 = (bf16[1,128,256]{1,2,0:T(8,128)(2,1)S(1)}, bf16[1,128,256]{1,2,0:T(8,128)(2,1)S(1)}, u32[]{:S(2)}, u32[]{:S(2)}) collective-permute-start(bf16[1,128,256]{1,2,0:T(8,128)(2,1)S(1)} %copy.113), channel_id=1, source_target_pairs={{0,2},{1,3},{2,4},{3,5},{4,6},{5,7},{8,10},{9,11},{10,12},{11,13},... | collective-permute-start | bytes 196616 | tf_op jit(solution)/shard_map/ppermute | solution.py:39
  13.1 1.5 %collective-permute-start.3 = (bf16[1,128,256]{1,2,0:T(8,128)(2,1)S(1)}, bf16[1,128,256]{1,2,0:T(8,128)(2,1)S(1)}, u32[]{:S(2)}, u32[]{:S(2)}) collective-permute-start(bf16[1,128,256]{1,2,0:T(8,128)(2,1)S(1)} %copy.113), channel_id=1, source_target_pairs={{0,1},{1,2},{2,3},{3,4},{4,5},{5,6},{6,7},{8,9},{9,10},{10,11},{11... | collective-permute-start | bytes 196616 | tf_op jit(solution)/shard_map/ppermute | solution.py:39
  14.5 3.9 %collective-permute-start = (bf16[1,128,256]{2,1,0:T(8,128)(2,1)}, bf16[1,128,256]{2,1,0:T(8,128)(2,1)S(1)}, u32[]{:S(2)}, u32[]{:S(2)}) collective-permute-start(bf16[1,128,256]{2,1,0:T(8,128)(2,1)} %param.13), channel_id=1, source_target_pairs={{0,2},{1,3},{2,4},{3,5},{4,6},{5,7},{8,10},{9,11},{10,12},{11,13},... | collective-permute-start | bytes 196616 | tf_op jit(solution)/shard_map/ppermute | solution.py:39
  18.4 3.2 %collective-permute-start.1 = (bf16[1,128,256]{2,1,0:T(8,128)(2,1)}, bf16[1,128,256]{2,1,0:T(8,128)(2,1)S(1)}, u32[]{:S(2)}, u32[]{:S(2)}) collective-permute-start(bf16[1,128,256]{2,1,0:T(8,128)(2,1)} %param.13), channel_id=1, source_target_pairs={{0,1},{1,2},{2,3},{3,4},{4,5},{5,6},{6,7},{8,9},{9,10},{10,11},{11... | collective-permute-start | bytes 196616 | tf_op jit(solution)/shard_map/ppermute | solution.py:39
  21.6 0.9 reshape.302
  22.6 0.9 reshape.284
  23.4 0.7 convert_bitcast_fusion
  25.1 0.8 copy.108
  26.0 1.3 %copy.101 = bf16[1,128,1792]{1,2,0:T(8,128)(2,1)S(1)} copy(bf16[1,128,1792]{2,1,0:T(8,128)(2,1)} %param.11) | data formatting | bytes 917504 | tf_op args[0]
  27.5 1.5 %and_and_fusion = pred[2,128,384]{1,2,0:T(8,128)(4,1)} fusion(s32[128,384]{0,1:T(8,128)S(1)} %iota_subtract_fusion, s32[2]{0:T(128)} %param.15, pred[384]{0:T(512)(128)(4,1)S(1)} %add_compare_fusion, pred[128,384]{0,1:T(8,128)(4,1)S(1)} %broadcast_compare_fusion), kind=kLoop, calls=%fused_computation.54 | loop fusion | flops 294912 | bytes 344456 | tf_op jit(solution)/shard_map/and | solution.py:80
  29.0 1.1 fusion.23
  30.1 1.1 copy.119
  31.2 1.0 copy.124
  32.3 0.8 copy.112
  33.2 1.6 %fusion.5 = (f32[2,7,128]{2,1,0:T(8,128)S(1)}, f32[2,384,128,7]{2,1,3,0:T(8,128)S(1)}) fusion(pred[2,128,384]{1,2,0:T(8,128)(4,1)} %and_and_fusion, bf16[384,2,128,1]{0,2,3,1:T(8,128)(2,1)S(1)} %bitcast.263, bf16[128,2,7,128]{0,3,2,1:T(8,128)(2,1)S(1)} %bitcast.255), kind=kOutput, calls=%fused_computation.10 | convolution fusion | flops 178223360 | bytes 3513344 | tf_op jit(solution)/shard_map/nrghd,nmgd->nghrm/dot_general | solution.py:96
  35.3 0.9 fusion.7
  36.3 0.7 fusion.47
  37.0 1.7 %copy.195 = f32[1,128,256]{2,1,0:T(8,128)} copy(f32[1,128,256]{1,2,0:T(8,128)} %get-tuple-element.146) | data formatting | bytes 262144
  38.7 1.3 %collective-permute-start.6 = (f32[1,128,256]{2,1,0:T(8,128)}, f32[1,128,256]{2,1,0:T(8,128)}, u32[]{:S(2)}, u32[]{:S(2)}) collective-permute-start(f32[1,128,256]{2,1,0:T(8,128)} %copy.195), channel_id=1, source_target_pairs={{1,0},{2,1},{3,2},{4,3},{5,4},{6,5},{7,6},{9,8},{10,9},{11,10},{12... | collective-permute-start | bytes 393224 | tf_op jit(solution)/shard_map/ppermute | solution.py:39
  40.0 1.7 %copy.196 = f32[1,128,256]{2,1,0:T(8,128)} copy(f32[1,128,256]{1,2,0:T(8,128)} %get-tuple-element.147) | data formatting | bytes 262144
  41.6 1.3 %collective-permute-start.7 = (f32[1,128,256]{2,1,0:T(8,128)}, f32[1,128,256]{2,1,0:T(8,128)}, u32[]{:S(2)}, u32[]{:S(2)}) collective-permute-start(f32[1,128,256]{2,1,0:T(8,128)} %copy.196), channel_id=1, source_target_pairs={{2,0},{3,1},{4,2},{5,3},{6,4},{7,5},{10,8},{11,9},{12,10},{13,11},... | collective-permute-start | bytes 393224 | tf_op jit(solution)/shard_map/ppermute | solution.py:39
  42.9 0.8 copy.194
  43.6 7.1 %all-gather.5.cloned.1.call-done = f32[16,128,128]{2,1,0:T(8,128)} async-done(((f32[2,128,128]{2,1,0:T(8,128)}), f32[16,128,128]{2,1,0:T(8,128)}) %all-gather.5.cloned.1.call-update) | async-done | bytes 1048592 | tf_op jit(solution)/shard_map/all_gather | solution.py:26
  51.2 1.4 %multiply_reduce_fusion.3 = (f32[128,2,7]{0,2,1:T(8,128)S(1)}, f32[1,128,2,7,128]{1,4,3,2,0:T(8,128)S(1)}) fusion(f32[1,128,2,7,128]{1,4,3,2,0:T(8,128)S(1)} %convolution_bitcast_fusion.3, bf16[2,7,128,128]{2,3,1,0:T(8,128)(2,1)} %fusion.23, bf16[128,2,128]{2,0,1:T(8,128)(2,1)} %copy-done.4), kind=kOutput, calls=%fused_computation.48 | convolution fusion | flops 59406592 | bytes 2366464 | tf_op jit(solution)/shard_map/nghrs,nsge->nrghe/dot_general | solution.py:88
  52.6 2.7 %multiply_reduce_fusion = (f32[2,7,128]{2,1,0:T(8,128)}, f32[128,2,7]{0,2,1:T(8,128)S(1)}, f32[128,2,7]{0,2,1:T(8,128)}, bf16[1,128,2,7,128]{1,4,3,2,0:T(8,128)(2,1)}) fusion(f32[1,128,2,7,128]{1,4,3,2,0:T(8,128)S(1)} %bitcast.260, f32[1,128,2,7,128]{1,4,3,2,0:T(8,128)S(1)} %get-tuple-element.152, f32[128,2,7]{0,2,1:T(8,128)S(1)} %add_sqrt_fusion, ...), kind=kOutput, calls=%fused_computation.43 | convolution fusion | flops 182119168 | bytes 5391360 | tf_op jit(solution)/shard_map/nghrm,nmgd->nrghd/dot_general | solution.py:104
  55.9 0.8 copy.130
  56.8 2.9 %fusion.6 = bf16[2,7,128,384]{2,3,1,0:T(8,128)(2,1)S(1)} fusion(bf16[384,2,128,1]{0,2,3,1:T(8,128)(2,1)S(1)} %bitcast.276, bf16[128,2,7,128]{0,3,2,1:T(8,128)(2,1)S(1)} %bitcast.270, f32[2,7,128]{2,1,0:T(8,128)S(1)} %bitcast.277, f32[2,7,128]{2,1,0:T(8,128)S(1)} %copy-done.27, f32[2,7,128]{2,1,0:T(8,128)S(1)} %get-tuple-element.153, ...), kind=kOutput, calls=%fused_computation.11 | convolution fusion | flops 181665792 | bytes 4903936 | tf_op jit(solution)/shard_map/nrghd,nmgd->nghrm/dot_general | solution.py:153
  60.9 1.7 %copy.192 = f32[1,128,256]{2,1,0:T(8,128)} copy(f32[1,128,256]{1,2,0:T(8,128)} %get-tuple-element.149) | data formatting | bytes 262144
  62.6 1.3 %collective-permute-start.4 = (f32[1,128,256]{2,1,0:T(8,128)}, f32[1,128,256]{2,1,0:T(8,128)}, u32[]{:S(2)}, u32[]{:S(2)}) collective-permute-start(f32[1,128,256]{2,1,0:T(8,128)} %copy.192), channel_id=1, source_target_pairs={{1,0},{2,1},{3,2},{4,3},{5,4},{6,5},{7,6},{9,8},{10,9},{11,10},{12... | collective-permute-start | bytes 393224 | tf_op jit(solution)/shard_map/ppermute | solution.py:39
  63.9 0.8 copy.193
  64.7 1.3 %collective-permute-start.5 = (f32[1,128,256]{2,1,0:T(8,128)}, f32[1,128,256]{2,1,0:T(8,128)}, u32[]{:S(2)}, u32[]{:S(2)}) collective-permute-start(f32[1,128,256]{2,1,0:T(8,128)} %copy.193), channel_id=1, source_target_pairs={{2,0},{3,1},{4,2},{5,3},{6,4},{7,5},{10,8},{11,9},{12,10},{13,11},... | collective-permute-start | bytes 393224 | tf_op jit(solution)/shard_map/ppermute | solution.py:39
  65.9 0.8 copy.191
  67.6 1.2 fusion.20
  68.8 2.0 %copy.146 = bf16[1,128,1792]{2,1,0:T(8,128)(2,1)} copy(bf16[1,128,1792]{1,2,0:T(8,128)(2,1)} %bitcast.262) | data formatting | bytes 917504
  70.8 2.0 %copy.145 = bf16[1,128,1792]{2,1,0:T(8,128)(2,1)} copy(bf16[1,128,1792]{1,2,0:T(8,128)(2,1)} %bitcast.271) | data formatting | bytes 917504
  72.8 21.2 %psum.14 = f32[1792]{0:T(1024)S(1)} all-reduce(f32[1792]{0:T(1024)S(1)} %div.45), channel_id=1, replica_groups=mesh['dp'=4,'ctx'=8] {'ctx'}, use_global_device_ids=true, to_apply=%region_10.11 | all-reduce | flops 1792 | bytes 14336 | tf_op jit(solution)/shard_map/psum | solution.py:16
  94.1 12.4 %psum.15 = f32[1792]{0:T(1024)} all-reduce(f32[1792]{0:T(1024)S(1)} %psum.14), channel_id=1, replica_groups=mesh['dp'=4,'ctx'=8] {'dp'}, use_global_device_ids=true, to_apply=%region_11.12 | all-reduce | flops 1792 | bytes 14336 | tf_op jit(solution)/shard_map/psum | solution.py:16
  107.2 6.8 %while.23 = (s32[]{:T(128)}, f32[1,2,128,128]{3,2,1,0:T(8,128)S(1)}, s32[]{:T(128)}, f32[8,1,2,128,128]{4,3,2,1,0:T(8,128)}, s32[]{:T(128)}, /*index=5*/s32[]{:T(128)}, s32[]{:T(128)}, s32[]{:T(128)}) while((s32[]{:T(128)}, f32[1,2,128,128]{3,2,1,0:T(8,128)S(1)}, s32[]{:T(128)}, f32[8,1,2,128,128]{4,3,2,1,0:T(8,128)}, s32[]{:T(128)}, ...), condition=%wide.region_8.9_spmd, body=%wide.region_7.8_spmd.sunk | while | flops 32774 | bytes 393351 | solution.py:33
  107.2 0.9 bitcast_add_fusion.5
  108.1 0.9 bitcast_add_fusion.5
  109.1 0.9 bitcast_add_fusion.5
  110.1 0.9 bitcast_add_fusion.5
  111.0 0.9 bitcast_add_fusion.5
  112.0 0.9 bitcast_add_fusion.5
  113.0 0.9 bitcast_add_fusion.5
  114.6 1.6 %add_convert_fusion.1 = bf16[1,128,256]{2,1,0:T(8,128)(2,1)} fusion(f32[1,128,256]{2,1,0:T(8,128)} %collective-permute-done.6, f32[1,128,256]{2,1,0:T(8,128)} %collective-permute-done.7, f32[1,128,256]{2,1,0:T(8,128)S(1)} %copy.142, f32[1,128,256]{2,1,0:T(8,128)S(1)} %copy-done.16), kind=kLoop, calls=%fused_computation.60 | loop fusion | flops 131072 | bytes 589824 | tf_op jit(solution)/shard_map/convert_element_type | solution.py:190
  116.2 1.6 %add_convert_fusion.2 = bf16[1,128,256]{2,1,0:T(8,128)(2,1)} fusion(f32[1,128,256]{2,1,0:T(8,128)} %collective-permute-done.4, f32[1,128,256]{2,1,0:T(8,128)} %collective-permute-done.5, f32[1,128,256]{2,1,0:T(8,128)S(1)} %copy.134, f32[1,128,256]{2,1,0:T(8,128)S(1)} %copy-done.17), kind=kLoop, calls=%fused_computation.61 | loop fusion | flops 131072 | bytes 589824 | tf_op jit(solution)/shard_map/convert_element_type | solution.py:185
  (108 shorter events, 6.3 us)
Async XLA Ops:
  7.2 22.9 %copy-start.3 = (bf16[1,128,1792]{2,1,0:T(8,128)(2,1)S(1)}, bf16[1,128,1792]{2,1,0:T(8,128)(2,1)}, u32[]{:S(2)}) copy-start(bf16[1,128,1792]{2,1,0:T(8,128)(2,1)} %param.17) | copy-start | bytes 1376260
  7.2 43.6 %all-gather.5.cloned.1.call-start = ((), (), s32[]{:S(2)}) async-start(), calls=%async_computation | async-start | bytes 1179648 | tf_op jit(solution)/shard_map/all_gather | solution.py:26
  8.2 24.9 %collective-permute-start.2 = (bf16[1,128,256]{1,2,0:T(8,128)(2,1)S(1)}, bf16[1,128,256]{1,2,0:T(8,128)(2,1)S(1)}, u32[]{:S(2)}, u32[]{:S(2)}) collective-permute-start(bf16[1,128,256]{1,2,0:T(8,128)(2,1)S(1)} %copy.113), channel_id=1, source_target_pairs={{0,2},{1,3},{2,4},{3,5},{4,6},{5,7},{8,10},{9,11},{10,12},{11,13},... | collective-permute-start | bytes 196616 | tf_op jit(solution)/shard_map/ppermute | solution.py:39
  13.1 20.0 %collective-permute-start.3 = (bf16[1,128,256]{1,2,0:T(8,128)(2,1)S(1)}, bf16[1,128,256]{1,2,0:T(8,128)(2,1)S(1)}, u32[]{:S(2)}, u32[]{:S(2)}) collective-permute-start(bf16[1,128,256]{1,2,0:T(8,128)(2,1)S(1)} %copy.113), channel_id=1, source_target_pairs={{0,1},{1,2},{2,3},{3,4},{4,5},{5,6},{6,7},{8,9},{9,10},{10,11},{11... | collective-permute-start | bytes 196616 | tf_op jit(solution)/shard_map/ppermute | solution.py:39
  14.5 17.7 %collective-permute-start = (bf16[1,128,256]{2,1,0:T(8,128)(2,1)}, bf16[1,128,256]{2,1,0:T(8,128)(2,1)S(1)}, u32[]{:S(2)}, u32[]{:S(2)}) collective-permute-start(bf16[1,128,256]{2,1,0:T(8,128)(2,1)} %param.13), channel_id=1, source_target_pairs={{0,2},{1,3},{2,4},{3,5},{4,6},{5,7},{8,10},{9,11},{10,12},{11,13},... | collective-permute-start | bytes 196616 | tf_op jit(solution)/shard_map/ppermute | solution.py:39
  18.4 13.8 %collective-permute-start.1 = (bf16[1,128,256]{2,1,0:T(8,128)(2,1)}, bf16[1,128,256]{2,1,0:T(8,128)(2,1)S(1)}, u32[]{:S(2)}, u32[]{:S(2)}) collective-permute-start(bf16[1,128,256]{2,1,0:T(8,128)(2,1)} %param.13), channel_id=1, source_target_pairs={{0,1},{1,2},{2,3},{3,4},{4,5},{5,6},{6,7},{8,9},{9,10},{10,11},{11... | collective-permute-start | bytes 196616 | tf_op jit(solution)/shard_map/ppermute | solution.py:39
  23.4 8.8 %copy-start.7 = (bf16[128,2,128]{2,1,0:T(2,128)(2,1)}, bf16[128,2,128]{2,1,0:T(2,128)(2,1)S(1)}, u32[]{:S(2)}) copy-start(bf16[128,2,128]{2,1,0:T(2,128)(2,1)S(1)} %reshape.284) | copy-start | bytes 196612
  24.1 1.8 %copy-start.23 = (f32[128,2]{0,1:T(2,128)}, f32[128,2]{0,1:T(2,128)S(1)}, u32[]{:S(2)}) copy-start(f32[128,2]{0,1:T(2,128)S(1)} %convert_bitcast_fusion) | copy-start | bytes 3076
  24.2 0.6 copy-start.4
  25.1 7.1 %copy-start.28 = (f32[1792]{0:T(1024)S(1)}, f32[1792]{0:T(1024)}, u32[]{:S(2)}) copy-start(f32[1792]{0:T(1024)} %param.16) | copy-start | bytes 21508
  25.1 7.1 %copy-start.20 = (bf16[1,128,256]{2,1,0:T(8,128)(2,1)S(1)}, bf16[1,128,256]{2,1,0:T(8,128)(2,1)}, u32[]{:S(2)}) copy-start(bf16[1,128,256]{2,1,0:T(8,128)(2,1)} %param.13) | copy-start | bytes 196612
  25.9 81.2 %all-gather.7.cloned.1.call-start = ((), (), s32[]{:S(2)}) async-start(), calls=%async_computation.1 | async-start | bytes 1179648 | tf_op jit(solution)/shard_map/all_gather | solution.py:26
  27.5 5.7 %copy-start.12 = (bf16[128,2,128,1]{0,2,3,1:T(8,128)(2,1)}, bf16[128,2,128,1]{0,2,3,1:T(8,128)(2,1)S(1)}, u32[]{:S(2)}) copy-start(bf16[128,2,128,1]{0,2,3,1:T(8,128)(2,1)S(1)} %copy.163) | copy-start | bytes 196612
  29.0 4.2 %copy-start.14 = (f32[128,128]{0,1:T(8,128)}, f32[128,128]{0,1:T(8,128)S(1)}, u32[]{:S(2)}) copy-start(f32[128,128]{0,1:T(8,128)S(1)} %fusion.38) | copy-start | bytes 196612
  32.2 2.5 %copy-start.9 = (pred[2,128,384]{1,2,0:T(8,128)(4,1)S(1)}, pred[2,128,384]{1,2,0:T(8,128)(4,1)}, u32[]{:S(2)}) copy-start(pred[2,128,384]{1,2,0:T(8,128)(4,1)} %and_and_fusion) | copy-start | bytes 294916
  33.1 2.2 %copy-start.18 = (bf16[1,128,1792]{1,2,0:T(8,128)(2,1)S(1)}, bf16[1,128,1792]{1,2,0:T(8,128)(2,1)}, u32[]{:S(2)}) copy-start(bf16[1,128,1792]{1,2,0:T(8,128)(2,1)} %copy.124) | copy-start | bytes 1376260
  34.7 17.9 %copy-start = (f32[2,384,128,7]{2,1,3,0:T(8,128)}, f32[2,384,128,7]{2,1,3,0:T(8,128)S(1)}, u32[]{:S(2)}) copy-start(f32[2,384,128,7]{2,1,3,0:T(8,128)S(1)} %get-tuple-element.154) | copy-start | bytes 8257540
  35.3 0.9 copy-start.25
  38.7 75.9 %collective-permute-start.6 = (f32[1,128,256]{2,1,0:T(8,128)}, f32[1,128,256]{2,1,0:T(8,128)}, u32[]{:S(2)}, u32[]{:S(2)}) collective-permute-start(f32[1,128,256]{2,1,0:T(8,128)} %copy.195), channel_id=1, source_target_pairs={{1,0},{2,1},{3,2},{4,3},{5,4},{6,5},{7,6},{9,8},{10,9},{11,10},{12... | collective-permute-start | bytes 393224 | tf_op jit(solution)/shard_map/ppermute | solution.py:39
  41.6 73.0 %collective-permute-start.7 = (f32[1,128,256]{2,1,0:T(8,128)}, f32[1,128,256]{2,1,0:T(8,128)}, u32[]{:S(2)}, u32[]{:S(2)}) collective-permute-start(f32[1,128,256]{2,1,0:T(8,128)} %copy.196), channel_id=1, source_target_pairs={{2,0},{3,1},{4,2},{5,3},{6,4},{7,5},{10,8},{11,9},{12,10},{13,11},... | collective-permute-start | bytes 393224 | tf_op jit(solution)/shard_map/ppermute | solution.py:39
  50.8 1.8 %copy-start.2 = (f32[1,128,1792]{1,2,0:T(8,128)S(1)}, f32[1,128,1792]{1,2,0:T(8,128)}, u32[]{:S(2)}) copy-start(f32[1,128,1792]{1,2,0:T(8,128)} %copy.119) | copy-start | bytes 2752516
  50.8 1.8 %copy-start.10 = (pred[2,128,384]{1,2,0:T(8,128)(4,1)S(1)}, pred[2,128,384]{1,2,0:T(8,128)(4,1)}, u32[]{:S(2)}) copy-start(pred[2,128,384]{1,2,0:T(8,128)(4,1)} %and_and_fusion) | copy-start | bytes 294916
  50.8 1.8 %copy-start.21 = (bf16[1,384,256]{1,2,0:T(8,128)(2,1)S(1)}, bf16[1,384,256]{1,2,0:T(8,128)(2,1)}, u32[]{:S(2)}) copy-start(bf16[1,384,256]{1,2,0:T(8,128)(2,1)} %copy.112) | copy-start | bytes 589828
  50.8 1.8 %copy-start.26 = (f32[2,7,128]{2,1,0:T(8,128)S(1)}, f32[2,7,128]{2,1,0:T(8,128)}, u32[]{:S(2)}) copy-start(f32[2,7,128]{2,1,0:T(8,128)} %copy-done.25) | copy-start | bytes 21508
  55.3 1.4 %copy-start.11 = (pred[2,128,384]{1,2,0:T(8,128)(4,1)S(1)}, pred[2,128,384]{1,2,0:T(8,128)(4,1)}, u32[]{:S(2)}) copy-start(pred[2,128,384]{1,2,0:T(8,128)(4,1)} %and_and_fusion) | copy-start | bytes 294916
  55.3 1.4 %copy-start.19 = (bf16[1,128,1792]{1,2,0:T(8,128)(2,1)S(1)}, bf16[1,128,1792]{1,2,0:T(8,128)(2,1)}, u32[]{:S(2)}) copy-start(bf16[1,128,1792]{1,2,0:T(8,128)(2,1)} %copy.124) | copy-start | bytes 1376260
  55.3 1.4 %copy-start.22 = (bf16[1,384,256]{1,2,0:T(8,128)(2,1)S(1)}, bf16[1,384,256]{1,2,0:T(8,128)(2,1)}, u32[]{:S(2)}) copy-start(bf16[1,384,256]{1,2,0:T(8,128)(2,1)} %copy.112) | copy-start | bytes 589828
  55.3 1.5 %copy-start.27 = (f32[2,7,128]{2,1,0:T(8,128)S(1)}, f32[2,7,128]{2,1,0:T(8,128)}, u32[]{:S(2)}) copy-start(f32[2,7,128]{2,1,0:T(8,128)} %copy-done.25) | copy-start | bytes 21508
  55.3 1.5 %copy-start.30 = (f32[128,2,7]{0,2,1:T(8,128)S(1)}, f32[128,2,7]{0,2,1:T(8,128)}, u32[]{:S(2)}) copy-start(f32[128,2,7]{0,2,1:T(8,128)} %get-tuple-element.127) | copy-start | bytes 21508
  59.7 7.0 %copy-start.5 = (bf16[128,2,128]{2,0,1:T(8,128)(2,1)S(1)}, bf16[128,2,128]{2,0,1:T(8,128)(2,1)}, u32[]{:S(2)}) copy-start(bf16[128,2,128]{2,0,1:T(8,128)(2,1)} %copy-done.4) | copy-start | bytes 196612
  59.7 7.0 %copy-start.15 = (f32[128,128]{0,1:T(8,128)S(1)}, f32[128,128]{0,1:T(8,128)}, u32[]{:S(2)}) copy-start(f32[128,128]{0,1:T(8,128)} %copy-done.14) | copy-start | bytes 196612
  59.7 7.3 %copy-start.13 = (bf16[128,2,128,1]{0,2,3,1:T(8,128)(2,1)S(1)}, bf16[128,2,128,1]{0,2,3,1:T(8,128)(2,1)}, u32[]{:S(2)}) copy-start(bf16[128,2,128,1]{0,2,3,1:T(8,128)(2,1)} %copy-done.12) | copy-start | bytes 196612
  62.6 53.6 %collective-permute-start.4 = (f32[1,128,256]{2,1,0:T(8,128)}, f32[1,128,256]{2,1,0:T(8,128)}, u32[]{:S(2)}, u32[]{:S(2)}) collective-permute-start(f32[1,128,256]{2,1,0:T(8,128)} %copy.192), channel_id=1, source_target_pairs={{1,0},{2,1},{3,2},{4,3},{5,4},{6,5},{7,6},{9,8},{10,9},{11,10},{12... | collective-permute-start | bytes 393224 | tf_op jit(solution)/shard_map/ppermute | solution.py:39
  64.7 51.6 %collective-permute-start.5 = (f32[1,128,256]{2,1,0:T(8,128)}, f32[1,128,256]{2,1,0:T(8,128)}, u32[]{:S(2)}, u32[]{:S(2)}) collective-permute-start(f32[1,128,256]{2,1,0:T(8,128)} %copy.193), channel_id=1, source_target_pairs={{2,0},{3,1},{4,2},{5,3},{6,4},{7,5},{10,8},{11,9},{12,10},{13,11},... | collective-permute-start | bytes 393224 | tf_op jit(solution)/shard_map/ppermute | solution.py:39
  67.5 5.3 %copy-start.29 = (f32[2,7,128]{2,1,0:T(8,128)S(1)}, f32[2,7,128]{2,1,0:T(8,128)}, u32[]{:S(2)}) copy-start(f32[2,7,128]{2,1,0:T(8,128)} %get-tuple-element.125) | copy-start | bytes 21508
  67.5 38.9 %copy-start.1 = (bf16[2,7,128,128]{2,3,1,0:T(8,128)(2,1)S(1)}, bf16[2,7,128,128]{2,3,1,0:T(8,128)(2,1)}, u32[]{:S(2)}) copy-start(bf16[2,7,128,128]{2,3,1,0:T(8,128)(2,1)} %fusion.23) | copy-start | bytes 1376260
  70.8 43.1 %copy-start.8 = (bf16[128,2,128]{2,1,0:T(2,128)(2,1)S(1)}, bf16[128,2,128]{2,1,0:T(2,128)(2,1)}, u32[]{:S(2)}) copy-start(bf16[128,2,128]{2,1,0:T(2,128)(2,1)} %copy-done.7) | copy-start | bytes 196612
  70.8 43.2 %copy-start.24 = (f32[128,2]{0,1:T(2,128)S(1)}, f32[128,2]{0,1:T(2,128)}, u32[]{:S(2)}) copy-start(f32[128,2]{0,1:T(2,128)} %copy-done.23) | copy-start | bytes 3076
  72.8 41.5 %copy-start.6 = (bf16[128,2,128]{2,0,1:T(8,128)(2,1)S(1)}, bf16[128,2,128]{2,0,1:T(8,128)(2,1)}, u32[]{:S(2)}) copy-start(bf16[128,2,128]{2,0,1:T(8,128)(2,1)} %copy-done.4) | copy-start | bytes 196612
  106.5 8.1 %copy-start.16 = (f32[1,128,256]{2,1,0:T(8,128)S(1)}, f32[1,128,256]{2,1,0:T(8,128)}, u32[]{:S(2)}) copy-start(f32[1,128,256]{2,1,0:T(8,128)} %copy.194) | copy-start | bytes 393220
  106.8 9.4 %copy-start.17 = (f32[1,128,256]{2,1,0:T(8,128)S(1)}, f32[1,128,256]{2,1,0:T(8,128)}, u32[]{:S(2)}) copy-start(f32[1,128,256]{2,1,0:T(8,128)} %copy.191) | copy-start | bytes 393220
Sparse Core Ops, SparseCore 0:
  26.0 24.7 all-gather.4
  56.8 32.2 all-gather.6
